TPU v7x, 256 devices: a whole 4x4x8 slice. The times are simulated.
256 devices in a mesh: rep: 32 (over x, y, core), tp: 8 (over z).
Axes of the slice: x: 4, y: 4, z: 8, core: 2. Of those that a mesh axis runs over, the one named last changes fastest.
Arguments:
- prompt_rows: bfloat16 [20480, 2048], P(('rep', 'tp')), may hold values from -6 to 6
- prompt_pieces: int32 [32, 640], P('rep'), may hold values from 0 to 9, never falling along the last dimension, each value on 1 to 320 neighbouring positions
- decode_rows: bfloat16 [1280, 2048], P('rep'), may hold values from -6 to 6
- request_ages: int32 [1280], P('rep'), may hold values from 2 to 127
- migrate_to: int32 [512, 1], P('rep'), may hold values from 0 to 31, as said below
- past_cache: bfloat16 [1280, 2, 128, 2048], P('rep', None, None, 'tp'), may hold values from -8 to 8
- norm_gain: float32 [2048], replicated, may hold values from 0.5 to 1.5
- norm_bias: float32 [2048], replicated, may hold values from -2 to 2
- qkv_weight: bfloat16 [3, 2048, 2048], P(None, None, 'tp'), may hold values from -0.125 to 0.125
- qkv_bias: float32 [3, 2048], P(None, 'tp'), may hold values from -4 to 4
- out_weight: bfloat16 [2048, 2048], P('tp'), may hold values from -0.125 to 0.125
- out_bias: float32 [2048], replicated, may hold values from -3 to 3
Outputs:
- prompt_out: bfloat16 [20480, 2048], P(('rep', 'tp'))
- prompt_cache: bfloat16 [2, 20480, 2048], P(None, 'rep', 'tp')
- kept_out: bfloat16 [768, 2048], P('rep')
- kept_cache: bfloat16 [768, 2, 128, 2048], P('rep', None, None, 'tp')
- moved_out: bfloat16 [1024, 2048], P('rep')
- moved_cache: bfloat16 [1024, 2, 128, 2048], P('rep', None, None, 'tp')
Inputs may be any that keep to these rules, and one draw needn't show every extreme that they name: `migrate_to`: the 16 requests that leave one replica name 16 different target replicas, and one target replica is named by every replica. `prompt_pieces`: piece numbers never fall along a replica's prompt tokens; a piece has at most 320 tokens, and some piece exactly that many.
All inputs are finite; a program needn't handle non-finite values.
Results may differ from a plain program's by a relative error of at most 0.014.
Values may be sent and summed in bfloat16 or wider, within the bound.
No kernel may reach another device: no remote copies, remote signals or barrier semaphores. Data moves between devices by JAX's collectives and lax.ppermute only.
A program may use at most 128 MiB of HBM per device.

v0:
```python
import jax
import jax.numpy as jnp
from jax import lax
from jax.sharding import PartitionSpec as P

HEAD_DIM = 128
CAP = 1
EPSILON = 1e-05


def layer_norm(values, norm_gain, norm_bias):
    wide = values.astype(jnp.float32)
    center = jnp.mean(wide, axis=-1, keepdims=True)
    spread = jnp.mean(jnp.square(wide - center), axis=-1, keepdims=True)
    scaled = (wide - center) * lax.rsqrt(spread + EPSILON)
    return (scaled * norm_gain + norm_bias).astype(jnp.bfloat16)


def decode_partial(
    rows, cache, live, position, norm_gain, norm_bias, qkv_weight, qkv_bias, out_weight
):
    count = rows.shape[0]
    width = qkv_weight.shape[2]
    heads_here = width // HEAD_DIM
    length = cache.shape[2]
    normed = layer_norm(rows, norm_gain, norm_bias)
    projected = jnp.einsum("rd,cde->cre", normed, qkv_weight, preferred_element_type=jnp.float32)
    queries = (projected[0] + qkv_bias[0]).astype(jnp.bfloat16).reshape(count, heads_here, HEAD_DIM)
    key_new = (projected[1] + qkv_bias[1]).astype(jnp.bfloat16)
    value_new = (projected[2] + qkv_bias[2]).astype(jnp.bfloat16)
    old_keys = cache[:, 0].reshape(count, length, heads_here, HEAD_DIM)
    old_values = cache[:, 1].reshape(count, length, heads_here, HEAD_DIM)
    scale = HEAD_DIM ** (-0.5)
    scores = (
        jnp.einsum("rhe,rlhe->rhl", queries, old_keys, preferred_element_type=jnp.float32) * scale
    )
    own = (
        jnp.sum(
            queries.astype(jnp.float32)
            * key_new.astype(jnp.float32).reshape(count, heads_here, HEAD_DIM),
            axis=-1,
        )
        * scale
    )
    scores = jnp.where(live[:, None, :], scores, -1e30)
    highest = jnp.maximum(jnp.max(scores, axis=-1), own)
    weights = jnp.exp(scores - highest[..., None])
    own_weight = jnp.exp(own - highest)
    total = jnp.sum(weights, axis=-1) + own_weight
    probs = (weights / total[..., None]).astype(jnp.bfloat16)
    own_prob = (own_weight / total).astype(jnp.bfloat16)
    context = jnp.einsum("rhl,rlhe->rhe", probs, old_values, preferred_element_type=jnp.float32)
    context = context + own_prob.astype(jnp.float32)[..., None] * value_new.astype(
        jnp.float32
    ).reshape(count, heads_here, HEAD_DIM)
    context = context.reshape(count, width).astype(jnp.bfloat16)
    partial_value = jnp.dot(context, out_weight, preferred_element_type=jnp.float32)
    written = (jnp.arange(length)[None, :] == position[:, None])[:, :, None]
    new_keys = jnp.where(written, key_new[:, None, :], cache[:, 0])
    new_values = jnp.where(written, value_new[:, None, :], cache[:, 1])
    return (partial_value, jnp.stack([new_keys, new_values], axis=1))


def on_device(
    prompt_rows,
    prompt_pieces,
    decode_rows,
    request_ages,
    migrate_to,
    past_cache,
    norm_gain,
    norm_bias,
    qkv_weight,
    qkv_bias,
    out_weight,
    out_bias,
):
    rep_count = lax.axis_size("rep")
    width = qkv_weight.shape[2]
    heads_here = width // HEAD_DIM
    length = past_cache.shape[2]
    leaving = migrate_to.shape[0]
    staying = decode_rows.shape[0] - leaving
    slot_count = rep_count * CAP
    normed = layer_norm(lax.all_gather(prompt_rows, "tp", axis=0, tiled=True), norm_gain, norm_bias)
    projected = jnp.einsum("rd,cde->cre", normed, qkv_weight, preferred_element_type=jnp.float32)
    total_rows = projected.shape[1]
    queries = (projected[0] + qkv_bias[0]).astype(jnp.bfloat16)
    key_rows = (projected[1] + qkv_bias[1]).astype(jnp.bfloat16)
    value_rows = (projected[2] + qkv_bias[2]).astype(jnp.bfloat16)
    head_q = queries.reshape(total_rows, heads_here, HEAD_DIM)
    head_k = key_rows.reshape(total_rows, heads_here, HEAD_DIM)
    head_v = value_rows.reshape(total_rows, heads_here, HEAD_DIM)
    scores = jnp.einsum(
        "qhe,khe->hqk", head_q, head_k, preferred_element_type=jnp.float32
    ) * HEAD_DIM ** (-0.5)
    pieces = prompt_pieces[0]
    position = jnp.arange(total_rows)
    allowed = (pieces[:, None] == pieces[None, :]) & (position[None, :] <= position[:, None])
    scores = jnp.where(allowed[None], scores, -1e30)
    highest = jnp.max(scores, axis=-1, keepdims=True)
    weights = jnp.exp(scores - highest)
    probs = (weights / jnp.sum(weights, axis=-1, keepdims=True)).astype(jnp.bfloat16)
    context = jnp.einsum("hqk,khe->qhe", probs, head_v, preferred_element_type=jnp.float32)
    context = context.reshape(total_rows, width).astype(jnp.bfloat16)
    attended = lax.psum_scatter(
        jnp.dot(context, out_weight, preferred_element_type=jnp.float32).astype(jnp.bfloat16),
        "tp",
        scatter_dimension=0,
        tiled=True,
    ).astype(jnp.float32)
    prompt_out = (prompt_rows.astype(jnp.float32) + attended + out_bias).astype(jnp.bfloat16)
    prompt_cache = jnp.stack([key_rows, value_rows])
    targets = migrate_to[:, 0]
    onehot = (targets[:, None] == jnp.arange(rep_count)[None, :]).astype(jnp.float32)
    lower = (jnp.arange(leaving)[:, None] > jnp.arange(leaving)[None, :]).astype(jnp.float32)
    earlier = jnp.dot(lower, onehot)
    rank = jnp.sum(earlier * onehot, axis=1).astype(jnp.int32)
    slot = targets * CAP + rank
    placing = (jnp.arange(slot_count)[:, None] == slot[None, :]).astype(jnp.bfloat16)
    cells = jnp.arange(length)
    live = cells[None, :] < request_ages[:, None]
    partial_value, updated = decode_partial(
        decode_rows,
        past_cache,
        live,
        request_ages,
        norm_gain,
        norm_bias,
        qkv_weight,
        qkv_bias,
        out_weight,
    )
    summed = lax.psum(partial_value.astype(jnp.bfloat16), "tp").astype(jnp.float32)
    decode_out = (decode_rows.astype(jnp.float32) + summed + out_bias).astype(jnp.bfloat16)
    kept_out = decode_out[:staying]
    kept_cache = updated[:staying]
    send_cache = jnp.einsum(
        "so,oklh->sklh", placing, updated[staying:], preferred_element_type=jnp.float32
    ).astype(jnp.bfloat16)
    send_rows = jnp.dot(placing, decode_out[staying:], preferred_element_type=jnp.float32).astype(
        jnp.bfloat16
    )
    moved_cache, moved_out = (
        lax.all_to_all(send_cache, "rep", split_axis=0, concat_axis=0, tiled=True),
        lax.all_to_all(send_rows, "rep", split_axis=0, concat_axis=0, tiled=True),
    )
    return (prompt_out, prompt_cache, kept_out, kept_cache, moved_out, moved_cache)


def solution(mesh):
    placed = (
        P(("rep", "tp"), None),
        P("rep", None),
        P("rep", None),
        P("rep"),
        P("rep", None),
        P("rep", None, None, "tp"),
        P(),
        P(),
        P(None, None, "tp"),
        P(None, "tp"),
        P("tp", None),
        P(),
    )
    return jax.shard_map(
        on_device,
        mesh=mesh,
        in_specs=placed,
        out_specs=(
            P(("rep", "tp"), None),
            P(None, "rep", "tp"),
            P("rep", None),
            P("rep", None, None, "tp"),
            P("rep", None),
            P("rep", None, None, "tp"),
        ),
        check_vma=False,
    )
```

profile of v0, /device:TPU:8, one launch (start us, length us, event | category | flops | bytes accessed | tf_op | source)
XLA Modules:
  0.0 225.0 jit_solution(8399299144730349695)
XLA Ops:
  8.0 0.8 iota_compare_fusion.1
  8.9 1.0 convert_reduce_fusion.1
  10.0 1.1 fusion.32
  11.1 1.6 convolution_bitcast_fusion
  13.1 5.5 %fusion.71 = (bf16[40,1,128,256]{3,2,1,0:T(8,128)(2,1)}, bf16[40,1,128,256]{3,2,1,0:T(8,128)(2,1)}) fusion(bf16[40,2,128,256]{3,2,1,0:T(8,128)(2,1)} %param.17), kind=kLoop, calls=%fused_computation.117 | loop fusion | bytes 10485760 | tf_op jit(solution)/shard_map/slice | solution.py:31
  18.6 4.4 %copy.84 = bf16[40,1,128,256]{2,3,0,1:T(8,128)(2,1)} copy(bf16[40,1,128,256]{3,2,1,0:T(8,128)(2,1)} %get-tuple-element.36) | data formatting | bytes 5242880 | tf_op jit(solution)/shard_map/reshape;squeeze | solution.py:31
  23.0 2.6 %fusion.53 = f32[40,2,1,128]{3,2,1,0:T(1,128)S(1)} fusion(bf16[40,128,2,128]{1,3,2,0:T(8,128)(2,1)} %bitcast.75, bf16[40,2,128,1]{2,1,0,3:T(2,128)(2,1)S(1)} %get-tuple-element.49), kind=kOutput, calls=%fused_computation.82 | convolution fusion | flops 2621440 | bytes 2682880 | tf_op jit(solution)/shard_map/rhe,rlhe->rhl/dot_general | solution.py:35
  26.1 4.9 %reshape.266 = bf16[40,128,2,128]{3,2,1,0:T(2,128)(2,1)} reshape(bf16[40,1,128,256]{3,2,1,0:T(8,128)(2,1)} %get-tuple-element.37) | data formatting | bytes 5242880 | tf_op jit(solution)/shard_map/reshape;squeeze | solution.py:32
  31.1 4.4 %fusion.11 = f32[40,2,1,128]{3,2,1,0:T(1,128)S(1)} fusion(bf16[40,2,128,1]{2,0,1,3:T(8,128)(2,1)S(1)} %fusion.59, bf16[40,128,2,128]{3,2,1,0:T(2,128)(2,1)} %reshape.266), kind=kOutput, calls=%fused_computation.20 | convolution fusion | flops 2621440 | bytes 2682880 | tf_op jit(solution)/shard_map/rhl,rlhe->rhe/dot_general | solution.py:52
  35.7 1.0 convolution_convert_fusion.2
  37.2 1.0 fusion.23
  38.3 8.5 %broadcast_select_fusion = (bf16[40,1,128,256]{3,0,2,1:T(8,128)(2,1)}, bf16[40,1,128,256]{3,0,2,1:T(8,128)(2,1)}) fusion(pred[40,128]{0,1:T(8,128)(4,1)S(1)} %get-tuple-element.57, bf16[40,256]{1,0:T(8,128)(2,1)S(1)} %get-tuple-element.43, bf16[40,1,128,256]{3,2,1,0:T(8,128)(2,1)} %get-tuple-element.37, bf16[40,1,128,256]{3,2,1,0:T(8,128)(2,1)} %get-tuple-element.36, ...), kind=kLoop, calls=%fused_computation.26 | loop fusion | flops 2621440 | bytes 10531840 | tf_op jit(solution)/shard_map/jit(_where)/select_n | solution.py:60
  46.8 8.3 %all-gather.2.cloned.1.call-done = bf16[640,2048]{1,0:T(8,128)(2,1)} async-done(((bf16[80,2048]{1,0:T(8,128)(2,1)}), bf16[640,2048]{1,0:T(8,128)(2,1)}) %all-gather.2.cloned.1.call-update) | async-done | bytes 2621456 | tf_op jit(solution)/shard_map/all_gather | solution.py:85
  55.1 2.3 %convert_reduce_fusion = f32[640]{0:T(1024)S(1)} fusion(bf16[640,2048]{1,0:T(8,128)(2,1)} %all-gather.2.cloned.1.call-done), kind=kLoop, calls=%fused_computation.2 | loop fusion | flops 2620800 | bytes 2624000 | tf_op jit(solution)/shard_map/reduce_sum | solution.py:13
  57.6 0.8 fusion.3
  58.4 3.1 %fusion.25 = f32[3,640,256]{1,2,0:T(8,128)S(1)} fusion(bf16[3,2048,256]{2,1,0:T(8,128)(2,1)S(1)} %copy-done, bf16[640,2048]{1,0:T(8,128)(2,1)S(1)} %copy-done.3, f32[2048]{0:T(1024)S(1)} %copy-done.12, f32[2048]{0:T(1024)S(1)} %copy-done.13, f32[640]{0:T(1024)S(1)} %add_rsqrt_fusion, f32[640]{0:T(1024)S(1)} %broadcast_multiply_fusion), kind=kOutput, calls=%fused_computation.39 | convolution fusion | flops 2021130240 | bytes 7754752 | tf_op jit(solution)/shard_map/rd,cde->cre/dot_general | solution.py:86
  63.2 2.0 fusion.74
  66.4 2.4 %convolution_convert_fusion = bf16[640,2048]{1,0:T(8,128)(2,1)} fusion(bf16[640,256]{0,1:T(8,128)(2,1)S(1)} %bitcast.78, bf16[256,2048]{1,0:T(8,128)(2,1)S(1)} %copy-done.5), kind=kOutput, calls=%fused_computation.14 | convolution fusion | flops 672399360 | bytes 3997696 | tf_op jit(solution)/shard_map/dot_general | solution.py:107
  68.9 60.0 %all-reduce.2.cloned.1.call-done = bf16[40,2048]{1,0:T(8,128)(2,1)} async-done(((bf16[40,2048]{1,0:T(8,128)(2,1)}), bf16[40,2048]{1,0:T(8,128)(2,1)}) %all-reduce.2.cloned.1.call-update) | async-done | bytes 163856 | tf_op jit(solution)/shard_map/psum | solution.py:134
  128.8 1.0 fusion.37
  131.3 1.3 reduce.1
  132.6 1.6 reshape.267
  134.3 7.4 %all-to-all-start = ((bf16[32,2,1024]{2,1,0:T(2,128)(2,1)}), bf16[32,2,1024]{2,1,0:T(2,128)(2,1)S(1)}, u32[]{:S(2)}, u32[]{:S(2)}) async-start(bf16[32,2,1024]{2,1,0:T(2,128)(2,1)} %reshape.267), calls=%async_computation.1 | async-start | bytes 262144 | tf_op jit(solution)/shard_map/all_to_all | solution.py:146
  141.7 2.6 %convolution_convert_fusion.1 = bf16[32,2,128,256]{3,0,2,1:T(8,128)(2,1)S(1)} fusion(bf16[40,1,128,256]{3,0,2,1:T(8,128)(2,1)S(1)} %copy-done.2, bf16[40,1,128,256]{3,0,2,1:T(8,128)(2,1)} %get-tuple-element.51, s32[16]{0:T(128)S(1)} %convert_add_fusion.1), kind=kOutput, calls=%fused_computation.16 | convolution fusion | flops 73400832 | bytes 9437248 | tf_op jit(solution)/shard_map/so,oklh->sklh/dot_general | solution.py:138
  144.3 4.4 %copy.72 = bf16[32,2,128,256]{3,2,1,0:T(8,128)(2,1)} copy(bf16[32,2,128,256]{3,0,2,1:T(8,128)(2,1)S(1)} %convolution_convert_fusion.1) | data formatting | bytes 8388608 | tf_op jit(solution)/shard_map/convert_element_type | solution.py:140
  148.7 7.4 %all-to-all-start.1 = ((bf16[32,2,128,256]{3,2,1,0:T(8,128)(2,1)}), bf16[32,2,128,256]{3,2,1,0:T(8,128)(2,1)}, u32[]{:S(2)}, u32[]{:S(2)}) async-start(bf16[32,2,128,256]{3,2,1,0:T(8,128)(2,1)} %copy.72), calls=%async_computation.2 | async-start | bytes 8388608 | tf_op jit(solution)/shard_map/all_to_all | solution.py:145
  156.2 1.6 fusion.7
  157.8 2.4 %copy.74 = bf16[24,2,128,256]{3,2,1,0:T(8,128)(2,1)} copy(bf16[24,2,128,256]{3,0,2,1:T(8,128)(2,1)S(1)} %fusion.7) | data formatting | bytes 6291456
  161.6 49.1 %all-to-all-done.1 = bf16[32,2,128,256]{3,2,1,0:T(8,128)(2,1)} async-done(((bf16[32,2,128,256]{3,2,1,0:T(8,128)(2,1)}), bf16[32,2,128,256]{3,2,1,0:T(8,128)(2,1)}, u32[]{:S(2)}, u32[]{:S(2)}) %all-to-all-start.1) | async-done | bytes 4194336 | tf_op jit(solution)/shard_map/all_to_all | solution.py:145
  210.8 1.1 copy.73
  211.9 1.8 add_convert_fusion.2
  213.7 4.8 %copy.120 = bf16[32,2,128,256]{3,2,1,0:T(8,128)(2,1)} copy(bf16[32,2,128,256]{3,2,1,0:T(8,128)(2,1)} %all-to-all-done.1) | data formatting | bytes 8388608
  (76 shorter events, 8.5 us)
Async XLA Ops:
  7.2 4.0 %copy-start = (bf16[3,2048,256]{2,1,0:T(8,128)(2,1)S(1)}, bf16[3,2048,256]{2,1,0:T(8,128)(2,1)}, u32[]{:S(2)}) copy-start(bf16[3,2048,256]{2,1,0:T(8,128)(2,1)} %param.20) | copy-start | bytes 9437188
  7.2 5.7 %copy-start.15 = (f32[3,256]{1,0:T(4,128)S(1)}, f32[3,256]{1,0:T(4,128)}, u32[]{:S(2)}) copy-start(f32[3,256]{1,0:T(4,128)} %param.21) | copy-start | bytes 9220
  7.2 47.9 %all-gather.2.cloned.1.call-start = ((), (), s32[]{:S(2)}) async-start(), calls=%async_computation.3 | async-start | bytes 2949120 | tf_op jit(solution)/shard_map/all_gather | solution.py:85
  7.9 120.9 %all-reduce.2.cloned.1.call-start = ((), (), s32[]{:S(2)}) async-start(), calls=%async_computation.5 | async-start | bytes 327680 | tf_op jit(solution)/shard_map/psum | solution.py:134
  31.1 4.6 %copy-start.4 = (bf16[256,2048]{1,0:T(8,128)(2,1)S(1)}, bf16[256,2048]{1,0:T(8,128)(2,1)}, u32[]{:S(2)}) copy-start(bf16[256,2048]{1,0:T(8,128)(2,1)} %param.22) | copy-start | bytes 3145732
  31.1 5.8 %copy-start.16 = (s32[16,1]{0,1:T(1,128)S(1)}, s32[16,1]{0,1:T(1,128)}, u32[]{:S(2)}) copy-start(s32[16,1]{0,1:T(1,128)} %param.16) | copy-start | bytes 196
  31.1 6.1 %copy-start.14 = (s32[1,640]{1,0:T(1,128)S(1)}, s32[1,640]{1,0:T(1,128)}, u32[]{:S(2)}) copy-start(s32[1,640]{1,0:T(1,128)} %param.13) | copy-start | bytes 7684
  36.6 175.2 %reduce-scatter.2.cloned.1.call-start = ((), (), s32[]{:S(2)}) async-start(), calls=%async_computation.4 | async-start | bytes 2949120 | tf_op jit(solution)/shard_map/reduce_scatter | solution.py:106
  46.8 11.7 %copy-start.12 = (f32[2048]{0:T(1024)S(1)}, f32[2048]{0:T(1024)}, u32[]{:S(2)}) copy-start(f32[2048]{0:T(1024)} %param.19) | copy-start | bytes 24580
  55.1 2.5 %copy-start.3 = (bf16[640,2048]{1,0:T(8,128)(2,1)S(1)}, bf16[640,2048]{1,0:T(8,128)(2,1)}, u32[]{:S(2)}) copy-start(bf16[640,2048]{1,0:T(8,128)(2,1)} %all-gather.2.cloned.1.call-done) | copy-start | bytes 7864324
  55.1 3.4 %copy-start.13 = (f32[2048]{0:T(1024)S(1)}, f32[2048]{0:T(1024)}, u32[]{:S(2)}) copy-start(f32[2048]{0:T(1024)} %param.18) | copy-start | bytes 24580
  62.2 1.0 copy-start.10
  65.2 1.2 copy-start.5
  66.4 62.4 %copy-start.6 = (bf16[40,2048]{1,0:T(8,128)(2,1)S(1)}, bf16[40,2048]{1,0:T(8,128)(2,1)}, u32[]{:S(2)}) copy-start(bf16[40,2048]{1,0:T(8,128)(2,1)} %param.14) | copy-start | bytes 491524
  66.4 62.4 %copy-start.11 = (f32[2048]{0:T(1024)S(1)}, f32[2048]{0:T(1024)}, u32[]{:S(2)}) copy-start(f32[2048]{0:T(1024)} %param.23) | copy-start | bytes 24580
  68.8 72.9 %copy-start.2 = (bf16[40,1,128,256]{3,0,2,1:T(8,128)(2,1)S(1)}, bf16[40,1,128,256]{3,0,2,1:T(8,128)(2,1)}, u32[]{:S(2)}) copy-start(bf16[40,1,128,256]{3,0,2,1:T(8,128)(2,1)} %get-tuple-element.50) | copy-start | bytes 7864324
  129.8 0.7 copy-start.8
  134.3 14.5 %all-to-all-start = ((bf16[32,2,1024]{2,1,0:T(2,128)(2,1)}), bf16[32,2,1024]{2,1,0:T(2,128)(2,1)S(1)}, u32[]{:S(2)}, u32[]{:S(2)}) async-start(bf16[32,2,1024]{2,1,0:T(2,128)(2,1)} %reshape.267), calls=%async_computation.1 | async-start | bytes 262144 | tf_op jit(solution)/shard_map/all_to_all | solution.py:146
  148.7 62.0 %all-to-all-start.1 = ((bf16[32,2,128,256]{3,2,1,0:T(8,128)(2,1)}), bf16[32,2,128,256]{3,2,1,0:T(8,128)(2,1)}, u32[]{:S(2)}, u32[]{:S(2)}) async-start(bf16[32,2,128,256]{3,2,1,0:T(8,128)(2,1)} %copy.72), calls=%async_computation.2 | async-start | bytes 8388608 | tf_op jit(solution)/shard_map/all_to_all | solution.py:145
  157.8 2.4 %copy-start.9 = (bf16[40,2048]{1,0:T(8,128)(2,1)S(1)}, bf16[40,2048]{1,0:T(8,128)(2,1)}, u32[]{:S(2)}) copy-start(bf16[40,2048]{1,0:T(8,128)(2,1)} %copy-done.8) | copy-start | bytes 491524
  160.1 51.7 %copy-start.7 = (bf16[80,2048]{1,0:T(8,128)(2,1)S(1)}, bf16[80,2048]{1,0:T(8,128)(2,1)}, u32[]{:S(2)}) copy-start(bf16[80,2048]{1,0:T(8,128)(2,1)} %param.12) | copy-start | bytes 983044
  213.7 4.9 %copy-start.1 = (bf16[3,2048,256]{2,1,0:T(8,128)(2,1)S(1)}, bf16[3,2048,256]{2,1,0:T(8,128)(2,1)}, u32[]{:S(2)}) copy-start(bf16[3,2048,256]{2,1,0:T(8,128)(2,1)} %param.20) | copy-start | bytes 9437188
Sparse Core Ops, SparseCore 0:
  9.8 45.1 all-gather.1
  58.0 70.8 all-reduce.1
  131.6 42.1 reduce-scatter.1
where the time goes:
time: 226 us; the launch traced here: 225 us
  waiting for transfers between devices  118 us (52%)
  local copies, waits for them, and re-layouts  34.1 us (15%)
  other arithmetic  24.3 us (11%)
  matrix products  19.4 us (9%)
  starting transfers between devices  15.1 us (7%)
  between operations  14.1 us (6%)
    psum x1, waiting for transfers between devices, on_device(): lax.psum(partial_value.astype(jnp.bfloat16), 'tp').astype(jnp.float32)  60 us
    all_to_all x1, waiting for transfers between devices, on_device(): lax.all_to_all(send_cache, 'rep', split_axis=0, concat_axis=0, tiled=True)  49.1 us
    unnamed x40, local copies, waits for them, and re-layouts  12.8 us
    select_n x1, other arithmetic, decode_partial(): new_values = jnp.where(written, value_new[:, None, :], cache[:, 1])  8.49 us
    all_gather x1, waiting for transfers between devices, on_device(): lax.all_gather(prompt_rows, 'tp', axis=0, tiled=True)  8.31 us
    all_to_all x1, starting transfers between devices, on_device(): lax.all_to_all(send_cache, 'rep', split_axis=0, concat_axis=0, tiled=True)  7.44 us
    all_to_all x1, starting transfers between devices, on_device(): lax.all_to_all(send_rows, 'rep', split_axis=0, concat_axis=0, tiled=True)  7.41 us
    slice x1, local copies, waits for them, and re-layouts, decode_partial(): old_keys = cache[:, 0].reshape(count, length, heads_here, HEAD_DIM)  5.54 us
  transfers between devices with their start and end apart: 5, of which 3 were waited for; matrix products, arithmetic and copies ran while one was open for 31% of the time, Pallas kernels for 0%

commit v1 on v0

--- a/solution.py
+++ b/solution.py
@@ -131,7 +131,9 @@
         qkv_bias,
         out_weight,
     )
-    summed = lax.psum(partial_value.astype(jnp.bfloat16), "tp").astype(jnp.float32)
+    summed = jnp.sum(lax.all_gather(partial_value.astype(jnp.bfloat16), "tp"), axis=0).astype(
+        jnp.float32
+    )
     decode_out = (decode_rows.astype(jnp.float32) + summed + out_bias).astype(jnp.bfloat16)
     kept_out = decode_out[:staying]
     kept_cache = updated[:staying]

time: 226 us -> 195 us (0.86)
  waiting for transfers between devices: 118 us -> 84.6 us
    psum x1 -> x0, waiting for transfers between devices: 60 us -> none  [on_device(): lax.psum(partial_value.astype(jnp.bfloat16), 'tp').astype(jnp.float32)]
    all_gather x0 -> x1, waiting for transfers between devices: none -> 26.5 us  [on_device(): lax.all_gather(partial_value.astype(jnp.bfloat16), 'tp')]
  transfers between devices with their start and end apart: 5 -> 5, of which waited for: 3 -> 3; matrix products, arithmetic and copies ran while one was open for 31% -> 37% of each run, Pallas kernels for 0% -> 0%
where the time goes in v1:
time: 195 us; the launch traced here: 194 us
  waiting for transfers between devices  84.6 us (43%)
  local copies, waits for them, and re-layouts  34.1 us (17%)
  other arithmetic  26.5 us (14%)
  matrix products  19.4 us (10%)
  starting transfers between devices  15.1 us (8%)
  between operations  14.1 us (7%)
    all_to_all x1, waiting for transfers between devices, on_device(): lax.all_to_all(send_cache, 'rep', split_axis=0, concat_axis=0, tiled=True)  49.1 us
    all_gather x1, waiting for transfers between devices, on_device(): lax.all_gather(partial_value.astype(jnp.bfloat16), 'tp')  26.5 us
    unnamed x40, local copies, waits for them, and re-layouts  12.8 us
    select_n x1, other arithmetic, decode_partial(): new_values = jnp.where(written, value_new[:, None, :], cache[:, 1])  8.49 us
    all_gather x1, waiting for transfers between devices, on_device(): lax.all_gather(prompt_rows, 'tp', axis=0, tiled=True)  8.31 us
    all_to_all x1, starting transfers between devices, on_device(): lax.all_to_all(send_cache, 'rep', split_axis=0, concat_axis=0, tiled=True)  7.44 us
    all_to_all x1, starting transfers between devices, on_device(): lax.all_to_all(send_rows, 'rep', split_axis=0, concat_axis=0, tiled=True)  7.4 us
    slice x1, local copies, waits for them, and re-layouts, decode_partial(): old_keys = cache[:, 0].reshape(count, length, heads_here, HEAD_DIM)  5.54 us
  transfers between devices with their start and end apart: 5, of which 3 were waited for; matrix products, arithmetic and copies ran while one was open for 37% of the time, Pallas kernels for 0%

profile of v1, /device:TPU:8, one launch (start us, length us, event | category | flops | bytes accessed | tf_op | source)
XLA Modules:
  0.0 193.8 jit_solution(13599956056124444567)
XLA Ops:
  8.0 0.8 iota_compare_fusion.1
  8.9 1.0 convert_reduce_fusion.1
  10.0 1.1 fusion.32
  11.1 1.6 convolution_bitcast_fusion
  13.1 5.5 %fusion.71 = (bf16[40,1,128,256]{3,2,1,0:T(8,128)(2,1)}, bf16[40,1,128,256]{3,2,1,0:T(8,128)(2,1)}) fusion(bf16[40,2,128,256]{3,2,1,0:T(8,128)(2,1)} %param.17), kind=kLoop, calls=%fused_computation.117 | loop fusion | bytes 10485760 | tf_op jit(solution)/shard_map/slice | solution.py:31
  18.6 4.4 %copy.84 = bf16[40,1,128,256]{2,3,0,1:T(8,128)(2,1)} copy(bf16[40,1,128,256]{3,2,1,0:T(8,128)(2,1)} %get-tuple-element.36) | data formatting | bytes 5242880 | tf_op jit(solution)/shard_map/reshape;squeeze | solution.py:31
  23.0 2.6 %fusion.53 = f32[40,2,1,128]{3,2,1,0:T(1,128)S(1)} fusion(bf16[40,128,2,128]{1,3,2,0:T(8,128)(2,1)} %bitcast.76, bf16[40,2,128,1]{2,1,0,3:T(2,128)(2,1)S(1)} %get-tuple-element.49), kind=kOutput, calls=%fused_computation.82 | convolution fusion | flops 2621440 | bytes 2682880 | tf_op jit(solution)/shard_map/rhe,rlhe->rhl/dot_general | solution.py:35
  26.1 4.9 %reshape.267 = bf16[40,128,2,128]{3,2,1,0:T(2,128)(2,1)} reshape(bf16[40,1,128,256]{3,2,1,0:T(8,128)(2,1)} %get-tuple-element.37) | data formatting | bytes 5242880 | tf_op jit(solution)/shard_map/reshape;squeeze | solution.py:32
  31.1 4.4 %fusion.11 = f32[40,2,1,128]{3,2,1,0:T(1,128)S(1)} fusion(bf16[40,2,128,1]{2,0,1,3:T(8,128)(2,1)S(1)} %fusion.59, bf16[40,128,2,128]{3,2,1,0:T(2,128)(2,1)} %reshape.267), kind=kOutput, calls=%fused_computation.20 | convolution fusion | flops 2621440 | bytes 2682880 | tf_op jit(solution)/shard_map/rhl,rlhe->rhe/dot_general | solution.py:52
  35.7 1.0 convolution_convert_fusion.2
  37.2 1.0 fusion.23
  38.3 8.5 %broadcast_select_fusion = (bf16[40,1,128,256]{3,0,2,1:T(8,128)(2,1)}, bf16[40,1,128,256]{3,0,2,1:T(8,128)(2,1)}) fusion(pred[40,128]{0,1:T(8,128)(4,1)S(1)} %get-tuple-element.57, bf16[40,256]{1,0:T(8,128)(2,1)S(1)} %get-tuple-element.43, bf16[40,1,128,256]{3,2,1,0:T(8,128)(2,1)} %get-tuple-element.37, bf16[40,1,128,256]{3,2,1,0:T(8,128)(2,1)} %get-tuple-element.36, ...), kind=kLoop, calls=%fused_computation.26 | loop fusion | flops 2621440 | bytes 10531840 | tf_op jit(solution)/shard_map/jit(_where)/select_n | solution.py:60
  46.8 8.3 %all-gather.4.cloned.1.call-done = bf16[640,2048]{1,0:T(8,128)(2,1)} async-done(((bf16[80,2048]{1,0:T(8,128)(2,1)}), bf16[640,2048]{1,0:T(8,128)(2,1)}) %all-gather.4.cloned.1.call-update) | async-done | bytes 2621456 | tf_op jit(solution)/shard_map/all_gather | solution.py:85
  55.1 2.3 %convert_reduce_fusion = f32[640]{0:T(1024)S(1)} fusion(bf16[640,2048]{1,0:T(8,128)(2,1)} %all-gather.4.cloned.1.call-done), kind=kLoop, calls=%fused_computation.2 | loop fusion | flops 2620800 | bytes 2624000 | tf_op jit(solution)/shard_map/reduce_sum | solution.py:13
  58.4 3.1 %fusion.25 = f32[3,640,256]{1,2,0:T(8,128)S(1)} fusion(bf16[3,2048,256]{2,1,0:T(8,128)(2,1)S(1)} %copy-done, bf16[640,2048]{1,0:T(8,128)(2,1)S(1)} %copy-done.3, f32[2048]{0:T(1024)S(1)} %copy-done.12, f32[2048]{0:T(1024)S(1)} %copy-done.13, f32[640]{0:T(1024)S(1)} %add_rsqrt_fusion, f32[640]{0:T(1024)S(1)} %broadcast_multiply_fusion), kind=kOutput, calls=%fused_computation.39 | convolution fusion | flops 2021130240 | bytes 7754752 | tf_op jit(solution)/shard_map/rd,cde->cre/dot_general | solution.py:86
  63.2 2.0 %fusion.74 = (f32[2,640]{1,0:T(2,128)S(1)}, f32[2,640,640]{1,2,0:T(8,128)S(1)}) fusion(f32[2,640,640]{1,2,0:T(8,128)S(1)} %fusion.38, pred[640,640]{0,1:T(8,128)(4,1)S(1)} %copy-done.10), kind=kOutput, calls=%fused_computation.120 | output fusion | flops 4915839 | bytes 6968320 | tf_op jit(solution)/shard_map/sub | solution.py:102
  66.4 2.4 %convolution_convert_fusion = bf16[640,2048]{1,0:T(8,128)(2,1)} fusion(bf16[640,256]{0,1:T(8,128)(2,1)S(1)} %bitcast.80, bf16[256,2048]{1,0:T(8,128)(2,1)S(1)} %copy-done.5), kind=kOutput, calls=%fused_computation.14 | convolution fusion | flops 672399360 | bytes 3997696 | tf_op jit(solution)/shard_map/dot_general | solution.py:107
  68.9 26.5 %all-gather.6.cloned.1.call-done = bf16[320,2048]{1,0:T(8,128)(2,1)} async-done(((bf16[40,2048]{1,0:T(8,128)(2,1)}), bf16[320,2048]{1,0:T(8,128)(2,1)}) %all-gather.6.cloned.1.call-update) | async-done | bytes 1310736 | tf_op jit(solution)/shard_map/all_gather | solution.py:134
  95.4 2.2 %reduce_sum.91 = bf16[40,2048]{1,0:T(8,128)(2,1)} reduce(bf16[8,40,2048]{2,1,0:T(8,128)(2,1)} %bitcast.79, bf16[]{:T(256)} %constant.22.clone.1), dimensions={0}, to_apply=%region_10.11 | reduce | flops 573440 | bytes 1474562 | tf_op jit(solution)/shard_map/reduce_sum | solution.py:134
  97.6 1.0 fusion.37
  100.1 1.3 reduce.2
  101.4 1.6 reshape.268
  103.0 7.4 %all-to-all-start = ((bf16[32,2,1024]{2,1,0:T(2,128)(2,1)}), bf16[32,2,1024]{2,1,0:T(2,128)(2,1)S(1)}, u32[]{:S(2)}, u32[]{:S(2)}) async-start(bf16[32,2,1024]{2,1,0:T(2,128)(2,1)} %reshape.268), calls=%async_computation.1 | async-start | bytes 262144 | tf_op jit(solution)/shard_map/all_to_all | solution.py:148
  110.5 2.6 %convolution_convert_fusion.1 = bf16[32,2,128,256]{3,0,2,1:T(8,128)(2,1)S(1)} fusion(bf16[40,1,128,256]{3,0,2,1:T(8,128)(2,1)S(1)} %copy-done.2, bf16[40,1,128,256]{3,0,2,1:T(8,128)(2,1)} %get-tuple-element.51, s32[16]{0:T(128)S(1)} %convert_add_fusion.1), kind=kOutput, calls=%fused_computation.16 | convolution fusion | flops 73400832 | bytes 9437248 | tf_op jit(solution)/shard_map/so,oklh->sklh/dot_general | solution.py:140
  113.1 4.4 %copy.72 = bf16[32,2,128,256]{3,2,1,0:T(8,128)(2,1)} copy(bf16[32,2,128,256]{3,0,2,1:T(8,128)(2,1)S(1)} %convolution_convert_fusion.1) | data formatting | bytes 8388608 | tf_op jit(solution)/shard_map/convert_element_type | solution.py:142
  117.5 7.4 %all-to-all-start.1 = ((bf16[32,2,128,256]{3,2,1,0:T(8,128)(2,1)}), bf16[32,2,128,256]{3,2,1,0:T(8,128)(2,1)}, u32[]{:S(2)}, u32[]{:S(2)}) async-start(bf16[32,2,128,256]{3,2,1,0:T(8,128)(2,1)} %copy.72), calls=%async_computation.2 | async-start | bytes 8388608 | tf_op jit(solution)/shard_map/all_to_all | solution.py:147
  124.9 1.6 fusion.7
  126.5 2.4 %copy.74 = bf16[24,2,128,256]{3,2,1,0:T(8,128)(2,1)} copy(bf16[24,2,128,256]{3,0,2,1:T(8,128)(2,1)S(1)} %fusion.7) | data formatting | bytes 6291456
  130.4 49.1 %all-to-all-done.1 = bf16[32,2,128,256]{3,2,1,0:T(8,128)(2,1)} async-done(((bf16[32,2,128,256]{3,2,1,0:T(8,128)(2,1)}), bf16[32,2,128,256]{3,2,1,0:T(8,128)(2,1)}, u32[]{:S(2)}, u32[]{:S(2)}) %all-to-all-start.1) | async-done | bytes 4194336 | tf_op jit(solution)/shard_map/all_to_all | solution.py:147
  179.5 1.1 copy.73
  180.6 1.8 add_convert_fusion.2
  182.4 4.8 %copy.119 = bf16[32,2,128,256]{3,2,1,0:T(8,128)(2,1)} copy(bf16[32,2,128,256]{3,2,1,0:T(8,128)(2,1)} %all-to-all-done.1) | data formatting | bytes 8388608
  (77 shorter events, 9.3 us)
Async XLA Ops:
  7.2 4.0 %copy-start = (bf16[3,2048,256]{2,1,0:T(8,128)(2,1)S(1)}, bf16[3,2048,256]{2,1,0:T(8,128)(2,1)}, u32[]{:S(2)}) copy-start(bf16[3,2048,256]{2,1,0:T(8,128)(2,1)} %param.20) | copy-start | bytes 9437188
  7.2 5.7 %copy-start.15 = (f32[3,256]{1,0:T(4,128)S(1)}, f32[3,256]{1,0:T(4,128)}, u32[]{:S(2)}) copy-start(f32[3,256]{1,0:T(4,128)} %param.21) | copy-start | bytes 9220
  7.2 47.9 %all-gather.4.cloned.1.call-start = ((), (), s32[]{:S(2)}) async-start(), calls=%async_computation.3 | async-start | bytes 2949120 | tf_op jit(solution)/shard_map/all_gather | solution.py:85
  7.9 87.5 %all-gather.6.cloned.1.call-start = ((), (), s32[]{:S(2)}) async-start(), calls=%async_computation.5 | async-start | bytes 1474560 | tf_op jit(solution)/shard_map/all_gather | solution.py:134
  31.1 4.6 %copy-start.4 = (bf16[256,2048]{1,0:T(8,128)(2,1)S(1)}, bf16[256,2048]{1,0:T(8,128)(2,1)}, u32[]{:S(2)}) copy-start(bf16[256,2048]{1,0:T(8,128)(2,1)} %param.22) | copy-start | bytes 3145732
  31.1 5.8 %copy-start.16 = (s32[16,1]{0,1:T(1,128)S(1)}, s32[16,1]{0,1:T(1,128)}, u32[]{:S(2)}) copy-start(s32[16,1]{0,1:T(1,128)} %param.16) | copy-start | bytes 196
  31.1 6.1 %copy-start.14 = (s32[1,640]{1,0:T(1,128)S(1)}, s32[1,640]{1,0:T(1,128)}, u32[]{:S(2)}) copy-start(s32[1,640]{1,0:T(1,128)} %param.13) | copy-start | bytes 7684
  36.6 144.0 %reduce-scatter.2.cloned.1.call-start = ((), (), s32[]{:S(2)}) async-start(), calls=%async_computation.4 | async-start | bytes 2949120 | tf_op jit(solution)/shard_map/reduce_scatter | solution.py:106
  46.8 11.7 %copy-start.12 = (f32[2048]{0:T(1024)S(1)}, f32[2048]{0:T(1024)}, u32[]{:S(2)}) copy-start(f32[2048]{0:T(1024)} %param.19) | copy-start | bytes 24580
  55.1 2.5 %copy-start.3 = (bf16[640,2048]{1,0:T(8,128)(2,1)S(1)}, bf16[640,2048]{1,0:T(8,128)(2,1)}, u32[]{:S(2)}) copy-start(bf16[640,2048]{1,0:T(8,128)(2,1)} %all-gather.4.cloned.1.call-done) | copy-start | bytes 7864324
  55.1 3.4 %copy-start.13 = (f32[2048]{0:T(1024)S(1)}, f32[2048]{0:T(1024)}, u32[]{:S(2)}) copy-start(f32[2048]{0:T(1024)} %param.18) | copy-start | bytes 24580
  62.2 1.0 copy-start.10
  65.2 1.2 copy-start.5
  68.8 28.8 %copy-start.6 = (bf16[40,2048]{1,0:T(8,128)(2,1)S(1)}, bf16[40,2048]{1,0:T(8,128)(2,1)}, u32[]{:S(2)}) copy-start(bf16[40,2048]{1,0:T(8,128)(2,1)} %param.14) | copy-start | bytes 491524
  68.8 28.8 %copy-start.11 = (f32[2048]{0:T(1024)S(1)}, f32[2048]{0:T(1024)}, u32[]{:S(2)}) copy-start(f32[2048]{0:T(1024)} %param.23) | copy-start | bytes 24580
  68.8 41.6 %copy-start.2 = (bf16[40,1,128,256]{3,0,2,1:T(8,128)(2,1)S(1)}, bf16[40,1,128,256]{3,0,2,1:T(8,128)(2,1)}, u32[]{:S(2)}) copy-start(bf16[40,1,128,256]{3,0,2,1:T(8,128)(2,1)} %get-tuple-element.50) | copy-start | bytes 7864324
  98.6 0.7 copy-start.8
  103.0 14.5 %all-to-all-start = ((bf16[32,2,1024]{2,1,0:T(2,128)(2,1)}), bf16[32,2,1024]{2,1,0:T(2,128)(2,1)S(1)}, u32[]{:S(2)}, u32[]{:S(2)}) async-start(bf16[32,2,1024]{2,1,0:T(2,128)(2,1)} %reshape.268), calls=%async_computation.1 | async-start | bytes 262144 | tf_op jit(solution)/shard_map/all_to_all | solution.py:148
  117.5 62.0 %all-to-all-start.1 = ((bf16[32,2,128,256]{3,2,1,0:T(8,128)(2,1)}), bf16[32,2,128,256]{3,2,1,0:T(8,128)(2,1)}, u32[]{:S(2)}, u32[]{:S(2)}) async-start(bf16[32,2,128,256]{3,2,1,0:T(8,128)(2,1)} %copy.72), calls=%async_computation.2 | async-start | bytes 8388608 | tf_op jit(solution)/shard_map/all_to_all | solution.py:147
  126.5 2.4 %copy-start.9 = (bf16[40,2048]{1,0:T(8,128)(2,1)S(1)}, bf16[40,2048]{1,0:T(8,128)(2,1)}, u32[]{:S(2)}) copy-start(bf16[40,2048]{1,0:T(8,128)(2,1)} %copy-done.8) | copy-start | bytes 491524
  128.9 51.7 %copy-start.7 = (bf16[80,2048]{1,0:T(8,128)(2,1)S(1)}, bf16[80,2048]{1,0:T(8,128)(2,1)}, u32[]{:S(2)}) copy-start(bf16[80,2048]{1,0:T(8,128)(2,1)} %param.12) | copy-start | bytes 983044
  182.4 4.9 %copy-start.1 = (bf16[3,2048,256]{2,1,0:T(8,128)(2,1)S(1)}, bf16[3,2048,256]{2,1,0:T(8,128)(2,1)}, u32[]{:S(2)}) copy-start(bf16[3,2048,256]{2,1,0:T(8,128)(2,1)} %param.20) | copy-start | bytes 9437188
Sparse Core Ops, SparseCore 0:
  9.8 45.1 all-gather.3
  57.4 37.9 all-gather.5
  98.0 42.7 reduce-scatter.1
